TPU v7x, 512 devices: a whole 4x4x16 slice. The times are simulated.
512 devices in a mesh: comp: 32 (over z, core), feat: 16 (over x, y).
Axes of the slice: x: 4, y: 4, z: 16, core: 2. Of those that a mesh axis runs over, the one named last changes fastest.
Arguments:
- block_values: bfloat16 [32, 16, 24, 128, 128], P('comp', 'feat'), may hold values from -0.0625 to 0.0625
- block_rows: int32 [32, 16, 24], P('comp', 'feat'), may hold values from 0 to 15, as said below
- block_cols: int32 [32, 16, 24], P('comp', 'feat'), may hold values from 0 to 13, as said below
- block_counts: int32 [32, 16], P('comp', 'feat'), may hold values from 8 to 24, as said below
- right_side: float32 [65536, 128], P(('comp', 'feat')), may hold values from -6 to 6
- ridge: float32 [128], replicated, may hold values from 0.1 to 2
Outputs:
- solution: float32 [28672, 128], P('feat')
- residual: float32 [65536, 128], P(('comp', 'feat'))
Inputs may be any that keep to these rules, and one draw needn't show every extreme that they name: Within one device the listed (block_rows, block_cols) pairs of all 24 slots are distinct; block rows are very uneven in how many blocks they hold. `block_cols`: see block_rows. `block_counts`: slots at or beyond a device's count are ignored; some device is full in every draw.
All inputs are finite; a program needn't handle non-finite values.
Results may differ from a plain program's by a relative error of at most 0.0029.
Values may be sent and summed in bfloat16 or wider, within the bound.
No kernel may reach another device: no remote copies, remote signals or barrier semaphores. Data moves between devices by JAX's collectives and lax.ppermute only.
A program may use at most 64 MiB of HBM per device.

v0:
```python
import jax
import jax.numpy as jnp
from jax import lax
from jax.sharding import PartitionSpec as P

RB_DEV = 16
CB_DEV = 14
ITERS = 2


def reduce_over(partial, axis, parts):
    rows = partial.shape[0] // parts
    pieces = partial.reshape(parts, rows, *partial.shape[1:])
    return lax.all_to_all(pieces, axis, 0, 0, tiled=True).sum(0)


def total_over_mesh(stacked, n_comp, n_feat):
    spread = jnp.broadcast_to(stacked[None], (n_feat,) + stacked.shape)
    by_feat = lax.all_to_all(spread, "feat", 0, 0, tiled=True).sum(0)
    spread = jnp.broadcast_to(by_feat[None], (n_comp,) + stacked.shape)
    return lax.all_to_all(spread, "comp", 0, 0, tiled=True).sum(0)


def shards(block_values, block_rows, block_cols, block_counts, right_side, ridge, n_comp, n_feat):
    values = block_values[0, 0]
    slot_rows = block_rows[0, 0]
    slot_cols = block_cols[0, 0]
    count_of_slots = block_counts[0, 0]
    responses = right_side.shape[1]
    total_slot_number = values.shape[0]
    block_edge = values.shape[1]
    feat_rows = CB_DEV * block_edge
    own_rows = feat_rows // n_comp
    comp_index = lax.axis_index("comp")
    slot_live = (jnp.arange(total_slot_number) < count_of_slots).astype(jnp.float32)
    row_lookup_table = (jnp.arange(RB_DEV)[:, None] == slot_rows[None, :]).astype(
        jnp.float32
    ) * slot_live[None, :]
    col_table = (jnp.arange(CB_DEV)[:, None] == slot_cols[None, :]).astype(jnp.float32) * slot_live[
        None, :
    ]

    def backward(low_slab):
        row_slabs = low_slab.reshape(RB_DEV, block_edge, responses)
        selected = jnp.take(row_slabs, slot_rows, axis=0)
        block_products = jnp.einsum(
            "sij,sik->sjk", values, selected, preferred_element_type=jnp.float32
        )
        summed = jnp.einsum(
            "qs,sjk->qjk", col_table, block_products, precision=lax.Precision.HIGHEST
        )
        return summed.reshape(feat_rows, responses)

    def forward(direction):
        col_panels = direction.astype(jnp.bfloat16).reshape(CB_DEV, block_edge, responses)
        forward_selected = jnp.take(col_panels, slot_cols, axis=0)
        forward_block_products = jnp.einsum(
            "sij,sjk->sik", values, forward_selected, preferred_element_type=jnp.float32
        )
        forward_summed = jnp.einsum(
            "rs,sik->rik", row_lookup_table, forward_block_products, precision=lax.Precision.HIGHEST
        )
        return reduce_over(forward_summed.reshape(RB_DEV * block_edge, responses), "feat", n_feat)

    def slab_of(current):
        return lax.all_gather(current.astype(jnp.bfloat16), "feat", axis=0, tiled=True)

    core = comp_index % 2
    half_rows = feat_rows // 2
    part_rows = half_rows // n_comp
    siblings = [(i, i ^ 1) for i in range(n_comp)]

    def gradient_rows(current):
        partial = backward(slab_of(current))
        kept = lax.dynamic_slice_in_dim(partial, core * half_rows, half_rows, axis=0)
        sent = lax.dynamic_slice_in_dim(partial, (1 - core) * half_rows, half_rows, axis=0)
        chip_sum = kept + lax.ppermute(sent, "comp", siblings)
        pieces = chip_sum.reshape(n_comp, part_rows, chip_sum.shape[1])
        landed = lax.all_to_all(pieces, "comp", 0, 0, tiled=True)
        halves = landed.reshape(n_comp // 2, 2, part_rows, chip_sum.shape[1]).sum(0)
        return halves.reshape(own_rows, chip_sum.shape[1])

    def whole_of(gathered):
        split = gathered.reshape(n_comp, 2, part_rows, gathered.shape[-1])
        return split.transpose(1, 0, 2, 3).reshape(feat_rows, gathered.shape[-1])

    def own_part(full):
        split = full.reshape(2, n_comp, part_rows, full.shape[-1])
        mine = lax.dynamic_slice_in_dim(split, comp_index, 1, axis=1)
        return mine.reshape(own_rows, full.shape[-1])

    def col_sq(x):
        return jnp.sum(x * x, axis=0)

    residual = right_side
    gradient_own = gradient_rows(residual)
    direction = whole_of(lax.all_gather(gradient_own, "comp", axis=0, tiled=False))
    image_rows = forward(direction)
    energy, image_energy = total_over_mesh(
        jnp.stack([col_sq(gradient_own), col_sq(image_rows)]), n_comp, n_feat
    )
    step_size = energy / (image_energy + ridge * energy)
    solution = step_size * direction
    residual = residual - step_size * image_rows
    for _ in range(1, ITERS):
        gradient_own = gradient_rows(residual) - ridge * own_part(solution)
        gathered = lax.all_gather(
            jnp.concatenate([gradient_own, col_sq(gradient_own)[None]], axis=0),
            "comp",
            axis=0,
            tiled=False,
        )
        gradient = whole_of(gathered[:, :own_rows])
        comp_energy = jnp.sum(gathered[:, own_rows], axis=0)
        spread = jnp.broadcast_to(comp_energy[None, None], (n_feat, 1, responses))
        next_energy = lax.all_to_all(spread, "feat", 0, 0, tiled=True).sum(0)[0]
        direction = gradient + next_energy / energy * direction
        energy = next_energy
        image_rows = forward(direction)
        image_energy, direction_energy = total_over_mesh(
            jnp.stack([col_sq(image_rows), col_sq(own_part(direction))]), n_comp, n_feat
        )
        step_size = energy / (image_energy + ridge * direction_energy)
        solution = solution + step_size * direction
        residual = residual - step_size * image_rows
    return (solution, residual)


def solution(mesh):
    placed = (
        P("comp", "feat", None, None, None),
        P("comp", "feat", None),
        P("comp", "feat", None),
        P("comp", "feat"),
        P(("comp", "feat"), None),
        P(),
    )
    n_comp = mesh.shape["comp"]
    n_feat = mesh.shape["feat"]

    def body(*args):
        return shards(*args, n_comp=n_comp, n_feat=n_feat)

    return jax.shard_map(
        body,
        mesh=mesh,
        in_specs=placed,
        out_specs=(P("feat", None), P(("comp", "feat"), None)),
        check_vma=False,
    )
```

profile of v0, /device:TPU:1, one launch (start us, length us, event | category | flops | bytes accessed | tf_op | source)
XLA Modules:
  0.0 364.6 jit_solution(9498467656124753706)
XLA Ops:
  0.7 0.7 compare_and_fusion.1
  1.4 0.7 compare_select_fusion.1
  2.7 0.8 convert_element_type.24
  3.6 20.0 %all_gather.15 = bf16[2048,128]{1,0:T(8,128)(2,1)S(1)} all-gather(bf16[128,128]{1,0:T(8,128)(2,1)S(1)} %convert_element_type.24), channel_id=1, replica_groups=mesh['comp'=32,'feat'=16] {'feat'}, dimensions={0}, use_global_device_ids=true | all-gather | bytes 557056 | tf_op jit(solution)/shard_map/all_gather | solution.py:66
  23.5 0.7 gather_fusion
  24.3 1.7 convolution_bitcast_fusion.3
  25.9 2.0 copy.91
  27.9 1.0 fusion.30
  28.9 0.3 copy.92
  29.3 9.8 %collective-permute-start = (f32[896,128]{1,0:T(8,128)S(1)}, f32[896,128]{1,0:T(8,128)S(1)}, u32[]{:S(2)}, u32[]{:S(2)}) collective-permute-start(f32[896,128]{1,0:T(8,128)S(1)} %constant_dynamic-slice_fusion.1), channel_id=1, source_target_pairs={{0,16},{16,0},{32,48},{48,32},{64,80},{80,64},{96,112},{112,96},{1... | collective-permute-start | bytes 1376264 | tf_op jit(solution)/shard_map/ppermute | solution.py:77
  39.2 1.4 collective-permute-done
  40.6 0.8 reshape.111
  41.5 13.5 %all-to-all-start = ((f32[32,28,128]{2,1,0:T(8,128)}), f32[32,28,128]{2,1,0:T(8,128)S(1)}, u32[]{:S(2)}, u32[]{:S(2)}) async-start(f32[32,28,128]{2,1,0:T(8,128)} %reshape.111), calls=%async_computation | async-start | bytes 1048576 | tf_op jit(solution)/shard_map/all_to_all | solution.py:79
  55.0 33.5 %all-to-all-done = f32[32,28,128]{2,1,0:T(8,128)S(1)} async-done(((f32[32,28,128]{2,1,0:T(8,128)}), f32[32,28,128]{2,1,0:T(8,128)S(1)}, u32[]{:S(2)}, u32[]{:S(2)}) %all-to-all-start) | async-done | bytes 458784 | tf_op jit(solution)/shard_map/all_to_all | solution.py:79
  88.5 29.8 %all_gather.16 = f32[32,56,128]{2,1,0:T(8,128)S(1)} all-gather(f32[1,56,128]{2,1,0:T(8,128)S(1)} %all_gather_reshape.3), channel_id=1, replica_groups=mesh['comp'=32,'feat'=16] {'comp'}, dimensions={0}, use_global_device_ids=true | all-gather | bytes 946176 | tf_op jit(solution)/shard_map/all_gather | solution.py:97
  118.5 0.9 copy-done.2
  119.4 0.5 copy.94
  120.1 1.6 gather_fusion.1
  121.7 3.1 convolution_bitcast_fusion.2
  124.8 3.0 copy.96
  127.9 2.4 fusion.24
  130.3 1.3 copy.97
  131.6 4.8 %all-to-all-start.1 = ((f32[16,128,128]{2,1,0:T(8,128)}), f32[16,128,128]{2,1,0:T(8,128)S(1)}, u32[]{:S(2)}, u32[]{:S(2)}) async-start(f32[16,128,128]{2,1,0:T(8,128)} %copy.97), calls=%async_computation.1 | async-start | bytes 2097152 | tf_op jit(solution)/shard_map/all_to_all | solution.py:14
  136.4 16.1 %all-to-all-done.1 = f32[16,128,128]{2,1,0:T(8,128)S(1)} async-done(((f32[16,128,128]{2,1,0:T(8,128)}), f32[16,128,128]{2,1,0:T(8,128)S(1)}, u32[]{:S(2)}, u32[]{:S(2)}) %all-to-all-start.1) | async-done | bytes 1048608 | tf_op jit(solution)/shard_map/all_to_all | solution.py:14
  152.6 10.6 %all_to_all.45 = f32[16,2,128]{2,1,0:T(2,128)S(1)} all-to-all(f32[16,2,128]{2,1,0:T(2,128)S(1)} %broadcast_in_dim.30), channel_id=1, replica_groups=mesh['comp'=32,'feat'=16] {'feat'}, dimensions={0} | all-to-all | bytes 32768 | tf_op jit(solution)/shard_map/all_to_all | solution.py:19
  163.3 19.7 %all_to_all.46 = f32[32,2,128]{2,1,0:T(2,128)S(1)} all-to-all(f32[32,2,128]{2,1,0:T(2,128)S(1)} %broadcast_in_dim.31), channel_id=1, replica_groups=mesh['comp'=32,'feat'=16] {'comp'}, dimensions={0} | all-to-all | bytes 65536 | tf_op jit(solution)/shard_map/all_to_all | solution.py:21
  183.0 0.6 copy-done.8
  183.6 16.7 %all_gather.17 = bf16[2048,128]{1,0:T(8,128)(2,1)S(1)} all-gather(bf16[128,128]{1,0:T(8,128)(2,1)S(1)} %fusion.21), channel_id=1, replica_groups=mesh['comp'=32,'feat'=16] {'feat'}, dimensions={0}, use_global_device_ids=true | all-gather | bytes 557056 | tf_op jit(solution)/shard_map/all_gather | solution.py:66
  200.3 0.8 gather_fusion.2
  201.1 1.7 convolution_bitcast_fusion.1
  202.8 2.0 copy.102
  204.7 1.7 fusion.28
  206.4 0.3 copy.103
  206.7 8.6 %collective-permute-start.1 = (f32[896,128]{1,0:T(8,128)S(1)}, f32[896,128]{1,0:T(8,128)S(1)}, u32[]{:S(2)}, u32[]{:S(2)}) collective-permute-start(f32[896,128]{1,0:T(8,128)S(1)} %constant_dynamic-slice_fusion), channel_id=1, source_target_pairs={{0,16},{16,0},{32,48},{48,32},{64,80},{80,64},{96,112},{112,96},{1... | collective-permute-start | bytes 1376264 | tf_op jit(solution)/shard_map/ppermute | solution.py:77
  215.4 1.2 collective-permute-done.1
  216.7 0.8 reshape.118
  217.5 3.9 %all-to-all-start.4 = ((f32[32,28,128]{2,1,0:T(8,128)}), f32[32,28,128]{2,1,0:T(8,128)S(1)}, u32[]{:S(2)}, u32[]{:S(2)}) async-start(f32[32,28,128]{2,1,0:T(8,128)} %reshape.118), calls=%async_computation.4 | async-start | bytes 1048576 | tf_op jit(solution)/shard_map/all_to_all | solution.py:79
  221.4 1.0 dynamic-slice_multiply_fusion
  222.4 32.5 %all-to-all-done.4 = f32[32,28,128]{2,1,0:T(8,128)S(1)} async-done(((f32[32,28,128]{2,1,0:T(8,128)}), f32[32,28,128]{2,1,0:T(8,128)S(1)}, u32[]{:S(2)}, u32[]{:S(2)}) %all-to-all-start.4) | async-done | bytes 458784 | tf_op jit(solution)/shard_map/all_to_all | solution.py:79
  255.1 30.4 %all-gather.1 = f32[32,57,128]{2,1,0:T(8,128)S(1)} all-gather(f32[1,57,128]{2,1,0:T(8,128)S(1)} %maximum_bitcast_fusion), channel_id=2, replica_groups=mesh['comp'=32,'feat'=16] {'comp'}, dimensions={0}, use_global_device_ids=true | all-gather | bytes 963072 | tf_op jit(solution)/shard_map/all_gather | solution.py:107
  285.6 0.6 broadcast_in_dim.33
  286.2 4.0 %all-to-all-start.5 = ((f32[16,1,128]{2,1,0:T(1,128)}), f32[16,1,128]{2,1,0:T(1,128)S(1)}, u32[]{:S(2)}, u32[]{:S(2)}) async-start(f32[16,1,128]{2,1,0:T(1,128)} %broadcast_in_dim.33), calls=%async_computation.5 | async-start | bytes 16384 | tf_op jit(solution)/shard_map/all_to_all | solution.py:116
  290.5 0.9 copy-done.3
  291.4 0.5 copy.108
  292.0 1.0 reshape.124
  293.0 3.6 all-to-all-done.5
  296.6 1.6 add_convert_fusion
  298.2 1.6 gather_fusion.3
  299.7 3.1 convolution_bitcast_fusion
  302.9 3.0 copy.110
  305.9 2.4 fusion.22
  308.4 1.4 copy.111
  309.7 4.3 %all-to-all-start.6 = ((f32[16,128,128]{2,1,0:T(8,128)}), f32[16,128,128]{2,1,0:T(8,128)}, u32[]{:S(2)}, u32[]{:S(2)}) async-start(f32[16,128,128]{2,1,0:T(8,128)} %copy.111), calls=%async_computation.6 | async-start | bytes 2097152 | tf_op jit(solution)/shard_map/all_to_all | solution.py:14
  314.1 1.1 fusion.20
  315.2 14.1 %all-to-all-done.6 = f32[16,128,128]{2,1,0:T(8,128)} async-done(((f32[16,128,128]{2,1,0:T(8,128)}), f32[16,128,128]{2,1,0:T(8,128)}, u32[]{:S(2)}, u32[]{:S(2)}) %all-to-all-start.6) | async-done | bytes 1048608 | tf_op jit(solution)/shard_map/all_to_all | solution.py:14
  329.3 1.3 reduce_sum.148
  330.7 10.1 %all_to_all.47 = f32[16,2,128]{2,1,0:T(2,128)S(1)} all-to-all(f32[16,2,128]{2,1,0:T(2,128)S(1)} %broadcast_in_dim.34), channel_id=1, replica_groups=mesh['comp'=32,'feat'=16] {'feat'}, dimensions={0} | all-to-all | bytes 32768 | tf_op jit(solution)/shard_map/all_to_all | solution.py:19
  340.8 0.6 broadcast_in_dim.35
  341.5 8.1 %all-to-all-start.8 = ((f32[32,2,128]{2,1,0:T(2,128)}), f32[32,2,128]{2,1,0:T(2,128)S(1)}, u32[]{:S(2)}, u32[]{:S(2)}) async-start(f32[32,2,128]{2,1,0:T(2,128)} %broadcast_in_dim.35), calls=%async_computation.8 | async-start | bytes 65536 | tf_op jit(solution)/shard_map/all_to_all | solution.py:21
  349.5 1.0 reshape.115
  350.5 1.0 reshape.125
  351.5 10.1 %all-to-all-done.8 = f32[32,2,128]{2,1,0:T(2,128)S(1)} async-done(((f32[32,2,128]{2,1,0:T(2,128)}), f32[32,2,128]{2,1,0:T(2,128)S(1)}, u32[]{:S(2)}, u32[]{:S(2)}) %all-to-all-start.8) | async-done | bytes 32800 | tf_op jit(solution)/shard_map/all_to_all | solution.py:21
  361.7 0.6 multiply_subtract_fusion
  362.4 2.3 multiply_add_fusion
  (72 shorter events, 1.4 us)
Async XLA Ops:
  0.6 23.6 %copy-start = (bf16[1,1,24,128,128]{4,3,2,1,0:T(8,128)(2,1)S(1)}, bf16[1,1,24,128,128]{4,3,2,1,0:T(8,128)(2,1)}, u32[]{:S(2)}) copy-start(bf16[1,1,24,128,128]{4,3,2,1,0:T(8,128)(2,1)} %param.10) | copy-start | bytes 2359300
  1.4 24.5 %copy-start.15 = (pred[24]{0:T(512)(128)(4,1)}, pred[24]{0:T(512)(128)(4,1)S(1)}, u32[]{:S(2)}) copy-start(pred[24]{0:T(512)(128)(4,1)S(1)} %compare_and_fusion.1) | copy-start | bytes 76
  2.7 23.2 %copy-start.7 = (s32[1024]{0:T(1024)}, s32[1024]{0:T(1024)S(1)}, u32[]{:S(2)}) copy-start(s32[1024]{0:T(1024)S(1)} %pad_clamp_fusion.1) | copy-start | bytes 12292
  25.9 2.0 copy-start.10
  29.3 11.3 %collective-permute-start = (f32[896,128]{1,0:T(8,128)S(1)}, f32[896,128]{1,0:T(8,128)S(1)}, u32[]{:S(2)}, u32[]{:S(2)}) collective-permute-start(f32[896,128]{1,0:T(8,128)S(1)} %constant_dynamic-slice_fusion.1), channel_id=1, source_target_pairs={{0,16},{16,0},{32,48},{48,32},{64,80},{80,64},{96,112},{112,96},{1... | collective-permute-start | bytes 1376264 | tf_op jit(solution)/shard_map/ppermute | solution.py:77
  41.5 47.0 %all-to-all-start = ((f32[32,28,128]{2,1,0:T(8,128)}), f32[32,28,128]{2,1,0:T(8,128)S(1)}, u32[]{:S(2)}, u32[]{:S(2)}) async-start(f32[32,28,128]{2,1,0:T(8,128)} %reshape.111), calls=%async_computation | async-start | bytes 1048576 | tf_op jit(solution)/shard_map/all_to_all | solution.py:79
  55.0 66.7 %copy-start.13 = (pred[24]{0:T(512)(128)(4,1)}, pred[24]{0:T(512)(128)(4,1)S(1)}, u32[]{:S(2)}) copy-start(pred[24]{0:T(512)(128)(4,1)S(1)} %compare_and_fusion) | copy-start | bytes 76
  118.5 0.9 copy-start.2
  120.0 4.8 %copy-start.1 = (f32[14,128,128]{2,1,0:T(8,128)}, f32[14,128,128]{2,1,0:T(8,128)S(1)}, u32[]{:S(2)}) copy-start(f32[14,128,128]{2,1,0:T(8,128)S(1)} %reshape.114) | copy-start | bytes 2752516
  124.8 3.0 copy-start.11
  131.6 51.4 %copy-start.6 = (f32[128]{0:T(128)S(1)}, f32[128]{0:T(128)}, u32[]{:S(2)}) copy-start(f32[128]{0:T(128)} %param.15) | copy-start | bytes 1540
  131.6 52.0 %copy-start.5 = (f32[128,128]{1,0:T(8,128)S(1)}, f32[128,128]{1,0:T(8,128)}, u32[]{:S(2)}) copy-start(f32[128,128]{1,0:T(8,128)} %param.14) | copy-start | bytes 196612
  131.6 20.9 %all-to-all-start.1 = ((f32[16,128,128]{2,1,0:T(8,128)}), f32[16,128,128]{2,1,0:T(8,128)S(1)}, u32[]{:S(2)}, u32[]{:S(2)}) async-start(f32[16,128,128]{2,1,0:T(8,128)} %copy.97), calls=%async_computation.1 | async-start | bytes 2097152 | tf_op jit(solution)/shard_map/all_to_all | solution.py:14
  136.4 64.6 %copy-start.16 = (pred[24]{0:T(512)(128)(4,1)S(1)}, pred[24]{0:T(512)(128)(4,1)}, u32[]{:S(2)}) copy-start(pred[24]{0:T(512)(128)(4,1)} %copy-done.15) | copy-start | bytes 76
  183.0 0.6 copy-start.8
  206.7 9.9 %collective-permute-start.1 = (f32[896,128]{1,0:T(8,128)S(1)}, f32[896,128]{1,0:T(8,128)S(1)}, u32[]{:S(2)}, u32[]{:S(2)}) collective-permute-start(f32[896,128]{1,0:T(8,128)S(1)} %constant_dynamic-slice_fusion), channel_id=1, source_target_pairs={{0,16},{16,0},{32,48},{48,32},{64,80},{80,64},{96,112},{112,96},{1... | collective-permute-start | bytes 1376264 | tf_op jit(solution)/shard_map/ppermute | solution.py:77
  217.5 37.5 %all-to-all-start.4 = ((f32[32,28,128]{2,1,0:T(8,128)}), f32[32,28,128]{2,1,0:T(8,128)S(1)}, u32[]{:S(2)}, u32[]{:S(2)}) async-start(f32[32,28,128]{2,1,0:T(8,128)} %reshape.118), calls=%async_computation.4 | async-start | bytes 1048576 | tf_op jit(solution)/shard_map/all_to_all | solution.py:79
  286.2 10.4 %all-to-all-start.5 = ((f32[16,1,128]{2,1,0:T(1,128)}), f32[16,1,128]{2,1,0:T(1,128)S(1)}, u32[]{:S(2)}, u32[]{:S(2)}) async-start(f32[16,1,128]{2,1,0:T(1,128)} %broadcast_in_dim.33), calls=%async_computation.5 | async-start | bytes 16384 | tf_op jit(solution)/shard_map/all_to_all | solution.py:116
  290.5 0.9 copy-start.3
  291.4 5.2 %copy-start.9 = (f32[2,128]{1,0:T(2,128)S(1)}, f32[2,128]{1,0:T(2,128)}, u32[]{:S(2)}) copy-start(f32[2,128]{1,0:T(2,128)} %copy-done.8) | copy-start | bytes 3076
  296.6 3.2 copy-start.14
  302.9 3.0 copy-start.12
  309.7 19.6 %all-to-all-start.6 = ((f32[16,128,128]{2,1,0:T(8,128)}), f32[16,128,128]{2,1,0:T(8,128)}, u32[]{:S(2)}, u32[]{:S(2)}) async-start(f32[16,128,128]{2,1,0:T(8,128)} %copy.111), calls=%async_computation.6 | async-start | bytes 2097152 | tf_op jit(solution)/shard_map/all_to_all | solution.py:14
  341.5 20.2 %all-to-all-start.8 = ((f32[32,2,128]{2,1,0:T(2,128)}), f32[32,2,128]{2,1,0:T(2,128)S(1)}, u32[]{:S(2)}, u32[]{:S(2)}) async-start(f32[32,2,128]{2,1,0:T(2,128)} %broadcast_in_dim.35), calls=%async_computation.8 | async-start | bytes 65536 | tf_op jit(solution)/shard_map/all_to_all | solution.py:21
  350.5 11.8 %copy-start.4 = (f32[1792,128]{1,0:T(8,128)S(1)}, f32[1792,128]{1,0:T(8,128)}, u32[]{:S(2)}) copy-start(f32[1792,128]{1,0:T(8,128)} %reshape.115) | copy-start | bytes 2752516
where the time goes:
time: 366 us; the launch traced here: 365 us
  blocking collectives  137 us (37%)
  waiting for transfers between devices  113 us (31%)
  starting transfers between devices  57.1 us (16%)
  local copies, waits for them, and re-layouts  27.9 us (8%)
  matrix products  17.1 us (5%)
  other arithmetic  10.9 us (3%)
    all_to_all x2, waiting for transfers between devices, gradient_rows(): landed = lax.all_to_all(pieces, 'comp', 0, 0, tiled=True)  66 us
    all_gather x2, blocking collectives, slab_of(): lax.all_gather(current.astype(jnp.bfloat16), 'feat', axis=0, tiled=True)  36.6 us
    all_gather x1, blocking collectives, shards(): lax.all_gather(jnp.concatenate([gradient_own, col_sq(gradient_own)[None]]...  30.4 us
    all_to_all x2, waiting for transfers between devices, reduce_over(): return lax.all_to_all(pieces, axis, 0, 0, tiled=True).sum(0)  30.2 us
    all_gather x1, blocking collectives, shards(): lax.all_gather(gradient_own, 'comp', axis=0, tiled=False)  29.8 us
    all_to_all x2, blocking collectives, total_over_mesh(): by_feat = lax.all_to_all(spread, 'feat', 0, 0, tiled=True).sum(0)  20.7 us
    all_to_all x1, blocking collectives, total_over_mesh(): return lax.all_to_all(spread, 'comp', 0, 0, tiled=True).sum(0)  19.7 us
    ppermute x2, starting transfers between devices, gradient_rows(): chip_sum = kept + lax.ppermute(sent, 'comp', siblings)  18.5 us
  transfers between devices with their start and end apart: 8, of which 8 were waited for; matrix products, arithmetic and copies ran while one was open for 2% of the time, Pallas kernels for 0%

commit v1 on v0

--- a/solution.py
+++ b/solution.py
@@ -6,6 +6,13 @@
 RB_DEV = 16
 CB_DEV = 14
 ITERS = 2
+
+
+def all_by_exchange(array, axis, d):
+    count = lax.axis_size(axis)
+    blocks = jnp.stack([array for _ in range(count)])
+    blocks = lax.all_to_all(blocks, axis, split_axis=0, concat_axis=0)
+    return jnp.concatenate(blocks, axis=d)
 
 
 def reduce_over(partial, axis, parts):
@@ -63,7 +70,7 @@
         return reduce_over(forward_summed.reshape(RB_DEV * block_edge, responses), "feat", n_feat)
 
     def slab_of(current):
-        return lax.all_gather(current.astype(jnp.bfloat16), "feat", axis=0, tiled=True)
+        return all_by_exchange(current.astype(jnp.bfloat16), "feat", 0)
 
     core = comp_index % 2
     half_rows = feat_rows // 2

time: 366 us -> 349 us (0.954)
  blocking collectives: 137 us -> 111 us
  waiting for transfers between devices: 113 us -> 122 us
    all_gather x2 -> x0, blocking collectives: 36.6 us -> none  [slab_of(): lax.all_gather(current.astype(jnp.bfloat16), 'feat', axis=0, tiled=True)]
    all_to_all x0 -> x1, blocking collectives: none -> 11.7 us  [all_by_exchange(): blocks = lax.all_to_all(blocks, axis, split_axis=0, concat_axis=0)]
    all_to_all x0 -> x1, waiting for transfers between devices: none -> 8.31 us  [all_by_exchange(): blocks = lax.all_to_all(blocks, axis, split_axis=0, concat_axis=0)]
    all_to_all x0 -> x1, starting transfers between devices: none -> 7.58 us  [all_by_exchange(): blocks = lax.all_to_all(blocks, axis, split_axis=0, concat_axis=0)]
    ppermute x2, starting transfers between devices: 18.5 us -> 11.3 us  [gradient_rows(): chip_sum = kept + lax.ppermute(sent, 'comp', siblings)]
  transfers between devices with their start and end apart: 8 -> 9, of which waited for: 8 -> 9; matrix products, arithmetic and copies ran while one was open for 2% -> 2% of each run, Pallas kernels for 0% -> 0%
where the time goes in v1:
time: 349 us; the launch traced here: 348 us
  waiting for transfers between devices  122 us (35%)
  blocking collectives  111 us (32%)
  starting transfers between devices  57.6 us (17%)
  local copies, waits for them, and re-layouts  28.9 us (8%)
  matrix products  17.1 us (5%)
  other arithmetic  9.55 us (3%)
    all_to_all x2, waiting for transfers between devices, gradient_rows(): landed = lax.all_to_all(pieces, 'comp', 0, 0, tiled=True)  66 us
    all_to_all x2, waiting for transfers between devices, reduce_over(): return lax.all_to_all(pieces, axis, 0, 0, tiled=True).sum(0)  31.5 us
    all_gather x1, blocking collectives, shards(): lax.all_gather(jnp.concatenate([gradient_own, col_sq(gradient_own)[None]]...  30.4 us
    all_gather x1, blocking collectives, shards(): lax.all_gather(gradient_own, 'comp', axis=0, tiled=False)  29.8 us
    all_to_all x2, blocking collectives, total_over_mesh(): by_feat = lax.all_to_all(spread, 'feat', 0, 0, tiled=True).sum(0)  19.7 us
    all_to_all x1, blocking collectives, total_over_mesh(): return lax.all_to_all(spread, 'comp', 0, 0, tiled=True).sum(0)  19.4 us
    all_to_all x2, starting transfers between devices, gradient_rows(): landed = lax.all_to_all(pieces, 'comp', 0, 0, tiled=True)  19 us
    all_to_all x1, blocking collectives, all_by_exchange(): blocks = lax.all_to_all(blocks, axis, split_axis=0, concat_axis=0)  11.7 us
  transfers between devices with their start and end apart: 9, of which 9 were waited for; matrix products, arithmetic and copies ran while one was open for 2% of the time, Pallas kernels for 0%

profile of v1, /device:TPU:1, one launch (start us, length us, event | category | flops | bytes accessed | tf_op | source)
XLA Modules:
  0.0 348.1 jit_solution(8098220391912056413)
XLA Ops:
  0.7 0.9 convert_element_type.24
  1.6 0.9 stack.16
  2.5 7.6 %all-to-all-start = ((bf16[16,128,128]{2,1,0:T(8,128)(2,1)}), bf16[16,128,128]{2,1,0:T(8,128)(2,1)S(1)}, u32[]{:S(2)}, u32[]{:S(2)}) async-start(bf16[16,128,128]{2,1,0:T(8,128)(2,1)} %stack.16), calls=%async_computation | async-start | bytes 1048576 | tf_op jit(solution)/shard_map/all_to_all | solution.py:14
  10.8 8.3 %all-to-all-done = bf16[16,128,128]{2,1,0:T(8,128)(2,1)S(1)} async-done(((bf16[16,128,128]{2,1,0:T(8,128)(2,1)}), bf16[16,128,128]{2,1,0:T(8,128)(2,1)S(1)}, u32[]{:S(2)}, u32[]{:S(2)}) %all-to-all-start) | async-done | bytes 524320 | tf_op jit(solution)/shard_map/all_to_all | solution.py:14
  19.1 0.7 gather_fusion
  19.8 1.7 convolution_bitcast_fusion.3
  21.5 2.0 copy.91
  23.5 1.0 fusion.30
  24.5 0.3 copy.92
  24.9 5.8 %collective-permute-start = (f32[896,128]{1,0:T(8,128)S(1)}, f32[896,128]{1,0:T(8,128)S(1)}, u32[]{:S(2)}, u32[]{:S(2)}) collective-permute-start(f32[896,128]{1,0:T(8,128)S(1)} %constant_dynamic-slice_fusion.1), channel_id=1, source_target_pairs={{0,16},{16,0},{32,48},{48,32},{64,80},{80,64},{96,112},{112,96},{1... | collective-permute-start | bytes 1376264 | tf_op jit(solution)/shard_map/ppermute | solution.py:84
  30.7 1.4 collective-permute-done
  32.1 0.8 reshape.108
  33.0 15.1 %all-to-all-start.1 = ((f32[32,28,128]{2,1,0:T(8,128)}), f32[32,28,128]{2,1,0:T(8,128)S(1)}, u32[]{:S(2)}, u32[]{:S(2)}) async-start(f32[32,28,128]{2,1,0:T(8,128)} %reshape.108), calls=%async_computation.1 | async-start | bytes 1048576 | tf_op jit(solution)/shard_map/all_to_all | solution.py:86
  48.2 33.5 %all-to-all-done.1 = f32[32,28,128]{2,1,0:T(8,128)S(1)} async-done(((f32[32,28,128]{2,1,0:T(8,128)}), f32[32,28,128]{2,1,0:T(8,128)S(1)}, u32[]{:S(2)}, u32[]{:S(2)}) %all-to-all-start.1) | async-done | bytes 458784 | tf_op jit(solution)/shard_map/all_to_all | solution.py:86
  81.7 29.8 %all_gather.9 = f32[32,56,128]{2,1,0:T(8,128)S(1)} all-gather(f32[1,56,128]{2,1,0:T(8,128)S(1)} %all_gather_reshape.3), channel_id=1, replica_groups=mesh['comp'=32,'feat'=16] {'comp'}, dimensions={0}, use_global_device_ids=true | all-gather | bytes 946176 | tf_op jit(solution)/shard_map/all_gather | solution.py:104
  111.7 0.9 copy-done.2
  112.6 0.5 copy.94
  113.3 1.6 gather_fusion.1
  114.8 3.1 convolution_bitcast_fusion.2
  118.0 3.0 copy.96
  121.0 2.4 fusion.24
  123.4 1.3 copy.97
  124.7 3.8 %all-to-all-start.2 = ((f32[16,128,128]{2,1,0:T(8,128)}), f32[16,128,128]{2,1,0:T(8,128)S(1)}, u32[]{:S(2)}, u32[]{:S(2)}) async-start(f32[16,128,128]{2,1,0:T(8,128)} %copy.97), calls=%async_computation.2 | async-start | bytes 2097152 | tf_op jit(solution)/shard_map/all_to_all | solution.py:21
  128.6 17.4 %all-to-all-done.2 = f32[16,128,128]{2,1,0:T(8,128)S(1)} async-done(((f32[16,128,128]{2,1,0:T(8,128)}), f32[16,128,128]{2,1,0:T(8,128)S(1)}, u32[]{:S(2)}, u32[]{:S(2)}) %all-to-all-start.2) | async-done | bytes 1048608 | tf_op jit(solution)/shard_map/all_to_all | solution.py:21
  146.0 9.5 %all_to_all.55 = f32[16,2,128]{2,1,0:T(2,128)S(1)} all-to-all(f32[16,2,128]{2,1,0:T(2,128)S(1)} %broadcast_in_dim.30), channel_id=1, replica_groups=mesh['comp'=32,'feat'=16] {'feat'}, dimensions={0} | all-to-all | bytes 32768 | tf_op jit(solution)/shard_map/all_to_all | solution.py:26
  155.6 19.4 %all_to_all.56 = f32[32,2,128]{2,1,0:T(2,128)S(1)} all-to-all(f32[32,2,128]{2,1,0:T(2,128)S(1)} %broadcast_in_dim.31), channel_id=1, replica_groups=mesh['comp'=32,'feat'=16] {'comp'}, dimensions={0} | all-to-all | bytes 65536 | tf_op jit(solution)/shard_map/all_to_all | solution.py:28
  175.1 0.5 copy-done.8
  175.7 11.7 %all_to_all.57 = bf16[16,128,128]{2,1,0:T(8,128)(2,1)S(1)} all-to-all(bf16[16,128,128]{2,1,0:T(8,128)(2,1)S(1)} %stack.20), channel_id=1, replica_groups=mesh['comp'=32,'feat'=16] {'feat'}, dimensions={0} | all-to-all | bytes 1048576 | tf_op jit(solution)/shard_map/all_to_all | solution.py:14
  187.5 0.8 gather_fusion.2
  188.3 1.7 convolution_bitcast_fusion.1
  190.0 2.0 copy.102
  191.9 1.7 fusion.28
  193.6 0.3 copy.103
  194.0 5.5 %collective-permute-start.1 = (f32[896,128]{1,0:T(8,128)S(1)}, f32[896,128]{1,0:T(8,128)S(1)}, u32[]{:S(2)}, u32[]{:S(2)}) collective-permute-start(f32[896,128]{1,0:T(8,128)S(1)} %constant_dynamic-slice_fusion), channel_id=1, source_target_pairs={{0,16},{16,0},{32,48},{48,32},{64,80},{80,64},{96,112},{112,96},{1... | collective-permute-start | bytes 1376264 | tf_op jit(solution)/shard_map/ppermute | solution.py:84
  199.5 1.2 collective-permute-done.1
  200.8 0.8 reshape.114
  201.6 3.9 %all-to-all-start.6 = ((f32[32,28,128]{2,1,0:T(8,128)}), f32[32,28,128]{2,1,0:T(8,128)S(1)}, u32[]{:S(2)}, u32[]{:S(2)}) async-start(f32[32,28,128]{2,1,0:T(8,128)} %reshape.114), calls=%async_computation.6 | async-start | bytes 1048576 | tf_op jit(solution)/shard_map/all_to_all | solution.py:86
  205.5 1.0 dynamic-slice_multiply_fusion
  206.5 32.5 %all-to-all-done.6 = f32[32,28,128]{2,1,0:T(8,128)S(1)} async-done(((f32[32,28,128]{2,1,0:T(8,128)}), f32[32,28,128]{2,1,0:T(8,128)S(1)}, u32[]{:S(2)}, u32[]{:S(2)}) %all-to-all-start.6) | async-done | bytes 458784 | tf_op jit(solution)/shard_map/all_to_all | solution.py:86
  239.2 30.4 %all-gather.1 = f32[32,57,128]{2,1,0:T(8,128)S(1)} all-gather(f32[1,57,128]{2,1,0:T(8,128)S(1)} %maximum_bitcast_fusion), channel_id=2, replica_groups=mesh['comp'=32,'feat'=16] {'comp'}, dimensions={0}, use_global_device_ids=true | all-gather | bytes 963072 | tf_op jit(solution)/shard_map/all_gather | solution.py:114
  269.7 0.6 broadcast_in_dim.33
  270.3 3.5 all-to-all-start.7
  274.0 0.9 copy-done.3
  274.9 0.5 copy.108
  275.5 1.0 reshape.120
  276.5 3.5 %all-to-all-done.7 = f32[16,1,128]{2,1,0:T(1,128)S(1)} async-done(((f32[16,1,128]{2,1,0:T(1,128)}), f32[16,1,128]{2,1,0:T(1,128)S(1)}, u32[]{:S(2)}, u32[]{:S(2)}) %all-to-all-start.7) | async-done | bytes 8224 | tf_op jit(solution)/shard_map/all_to_all | solution.py:123
  280.1 1.6 add_convert_fusion
  281.6 1.6 gather_fusion.3
  283.2 3.1 convolution_bitcast_fusion
  286.3 3.0 copy.110
  289.4 2.4 fusion.22
  291.8 1.4 copy.111
  293.2 4.3 %all-to-all-start.8 = ((f32[16,128,128]{2,1,0:T(8,128)}), f32[16,128,128]{2,1,0:T(8,128)}, u32[]{:S(2)}, u32[]{:S(2)}) async-start(f32[16,128,128]{2,1,0:T(8,128)} %copy.111), calls=%async_computation.8 | async-start | bytes 2097152 | tf_op jit(solution)/shard_map/all_to_all | solution.py:21
  297.5 1.1 fusion.20
  298.7 14.1 %all-to-all-done.8 = f32[16,128,128]{2,1,0:T(8,128)} async-done(((f32[16,128,128]{2,1,0:T(8,128)}), f32[16,128,128]{2,1,0:T(8,128)}, u32[]{:S(2)}, u32[]{:S(2)}) %all-to-all-start.8) | async-done | bytes 1048608 | tf_op jit(solution)/shard_map/all_to_all | solution.py:21
  312.8 1.3 reduce_sum.148
  314.1 10.2 %all_to_all.58 = f32[16,2,128]{2,1,0:T(2,128)S(1)} all-to-all(f32[16,2,128]{2,1,0:T(2,128)S(1)} %broadcast_in_dim.34), channel_id=1, replica_groups=mesh['comp'=32,'feat'=16] {'feat'}, dimensions={0} | all-to-all | bytes 32768 | tf_op jit(solution)/shard_map/all_to_all | solution.py:26
  324.3 0.6 broadcast_in_dim.35
  325.0 8.1 %all-to-all-start.10 = ((f32[32,2,128]{2,1,0:T(2,128)}), f32[32,2,128]{2,1,0:T(2,128)S(1)}, u32[]{:S(2)}, u32[]{:S(2)}) async-start(f32[32,2,128]{2,1,0:T(2,128)} %broadcast_in_dim.35), calls=%async_computation.10 | async-start | bytes 65536 | tf_op jit(solution)/shard_map/all_to_all | solution.py:28
  333.0 1.0 reshape.112
  334.0 1.0 reshape.121
  335.0 10.1 %all-to-all-done.10 = f32[32,2,128]{2,1,0:T(2,128)S(1)} async-done(((f32[32,2,128]{2,1,0:T(2,128)}), f32[32,2,128]{2,1,0:T(2,128)S(1)}, u32[]{:S(2)}, u32[]{:S(2)}) %all-to-all-start.10) | async-done | bytes 32800 | tf_op jit(solution)/shard_map/all_to_all | solution.py:28
  345.2 0.6 multiply_subtract_fusion
  345.9 2.3 multiply_add_fusion
  (75 shorter events, 1.6 us)
Async XLA Ops:
  0.6 19.2 %copy-start = (bf16[1,1,24,128,128]{4,3,2,1,0:T(8,128)(2,1)S(1)}, bf16[1,1,24,128,128]{4,3,2,1,0:T(8,128)(2,1)}, u32[]{:S(2)}) copy-start(bf16[1,1,24,128,128]{4,3,2,1,0:T(8,128)(2,1)} %param.10) | copy-start | bytes 2359300
  0.6 9.4 %copy-start.11 = (s32[1,1,24]{2,1,0:T(1,128)S(1)}, s32[1,1,24]{2,1,0:T(1,128)}, u32[]{:S(2)}) copy-start(s32[1,1,24]{2,1,0:T(1,128)} %param.11) | copy-start | bytes 292
  2.5 16.7 %all-to-all-start = ((bf16[16,128,128]{2,1,0:T(8,128)(2,1)}), bf16[16,128,128]{2,1,0:T(8,128)(2,1)S(1)}, u32[]{:S(2)}, u32[]{:S(2)}) async-start(bf16[16,128,128]{2,1,0:T(8,128)(2,1)} %stack.16), calls=%async_computation | async-start | bytes 1048576 | tf_op jit(solution)/shard_map/all_to_all | solution.py:14
  10.8 10.7 %copy-start.7 = (s32[1024]{0:T(1024)}, s32[1024]{0:T(1024)S(1)}, u32[]{:S(2)}) copy-start(s32[1024]{0:T(1024)S(1)} %pad_clamp_fusion.1) | copy-start | bytes 12292
  10.8 10.7 %copy-start.15 = (pred[24]{0:T(512)(128)(4,1)}, pred[24]{0:T(512)(128)(4,1)S(1)}, u32[]{:S(2)}) copy-start(pred[24]{0:T(512)(128)(4,1)S(1)} %compare_and_fusion.1) | copy-start | bytes 76
  21.5 2.0 copy-start.10
  24.9 7.2 %collective-permute-start = (f32[896,128]{1,0:T(8,128)S(1)}, f32[896,128]{1,0:T(8,128)S(1)}, u32[]{:S(2)}, u32[]{:S(2)}) collective-permute-start(f32[896,128]{1,0:T(8,128)S(1)} %constant_dynamic-slice_fusion.1), channel_id=1, source_target_pairs={{0,16},{16,0},{32,48},{48,32},{64,80},{80,64},{96,112},{112,96},{1... | collective-permute-start | bytes 1376264 | tf_op jit(solution)/shard_map/ppermute | solution.py:84
  33.0 48.7 %all-to-all-start.1 = ((f32[32,28,128]{2,1,0:T(8,128)}), f32[32,28,128]{2,1,0:T(8,128)S(1)}, u32[]{:S(2)}, u32[]{:S(2)}) async-start(f32[32,28,128]{2,1,0:T(8,128)} %reshape.108), calls=%async_computation.1 | async-start | bytes 1048576 | tf_op jit(solution)/shard_map/all_to_all | solution.py:86
  48.1 66.7 %copy-start.13 = (pred[24]{0:T(512)(128)(4,1)}, pred[24]{0:T(512)(128)(4,1)S(1)}, u32[]{:S(2)}) copy-start(pred[24]{0:T(512)(128)(4,1)S(1)} %compare_and_fusion) | copy-start | bytes 76
  111.6 0.9 copy-start.2
  113.2 4.8 %copy-start.1 = (f32[14,128,128]{2,1,0:T(8,128)}, f32[14,128,128]{2,1,0:T(8,128)S(1)}, u32[]{:S(2)}) copy-start(f32[14,128,128]{2,1,0:T(8,128)S(1)} %reshape.111) | copy-start | bytes 2752516
  124.7 50.3 %copy-start.6 = (f32[128]{0:T(128)S(1)}, f32[128]{0:T(128)}, u32[]{:S(2)}) copy-start(f32[128]{0:T(128)} %param.15) | copy-start | bytes 1540
  124.7 50.3 %copy-start.5 = (f32[128,128]{1,0:T(8,128)S(1)}, f32[128,128]{1,0:T(8,128)}, u32[]{:S(2)}) copy-start(f32[128,128]{1,0:T(8,128)} %param.14) | copy-start | bytes 196612
  124.7 21.2 %all-to-all-start.2 = ((f32[16,128,128]{2,1,0:T(8,128)}), f32[16,128,128]{2,1,0:T(8,128)S(1)}, u32[]{:S(2)}, u32[]{:S(2)}) async-start(f32[16,128,128]{2,1,0:T(8,128)} %copy.97), calls=%async_computation.2 | async-start | bytes 2097152 | tf_op jit(solution)/shard_map/all_to_all | solution.py:21
  175.0 0.6 copy-start.8
  175.6 12.7 %copy-start.16 = (pred[24]{0:T(512)(128)(4,1)S(1)}, pred[24]{0:T(512)(128)(4,1)}, u32[]{:S(2)}) copy-start(pred[24]{0:T(512)(128)(4,1)} %copy-done.15) | copy-start | bytes 76
  194.0 6.8 %collective-permute-start.1 = (f32[896,128]{1,0:T(8,128)S(1)}, f32[896,128]{1,0:T(8,128)S(1)}, u32[]{:S(2)}, u32[]{:S(2)}) collective-permute-start(f32[896,128]{1,0:T(8,128)S(1)} %constant_dynamic-slice_fusion), channel_id=1, source_target_pairs={{0,16},{16,0},{32,48},{48,32},{64,80},{80,64},{96,112},{112,96},{1... | collective-permute-start | bytes 1376264 | tf_op jit(solution)/shard_map/ppermute | solution.py:84
  201.6 37.5 %all-to-all-start.6 = ((f32[32,28,128]{2,1,0:T(8,128)}), f32[32,28,128]{2,1,0:T(8,128)S(1)}, u32[]{:S(2)}, u32[]{:S(2)}) async-start(f32[32,28,128]{2,1,0:T(8,128)} %reshape.114), calls=%async_computation.6 | async-start | bytes 1048576 | tf_op jit(solution)/shard_map/all_to_all | solution.py:86
  270.3 9.8 %all-to-all-start.7 = ((f32[16,1,128]{2,1,0:T(1,128)}), f32[16,1,128]{2,1,0:T(1,128)S(1)}, u32[]{:S(2)}, u32[]{:S(2)}) async-start(f32[16,1,128]{2,1,0:T(1,128)} %broadcast_in_dim.33), calls=%async_computation.7 | async-start | bytes 16384 | tf_op jit(solution)/shard_map/all_to_all | solution.py:123
  274.0 0.9 copy-start.3
  274.9 5.1 %copy-start.9 = (f32[2,128]{1,0:T(2,128)S(1)}, f32[2,128]{1,0:T(2,128)}, u32[]{:S(2)}) copy-start(f32[2,128]{1,0:T(2,128)} %copy-done.8) | copy-start | bytes 3076
  280.1 3.2 copy-start.14
  286.3 3.0 copy-start.12
  293.2 19.6 %all-to-all-start.8 = ((f32[16,128,128]{2,1,0:T(8,128)}), f32[16,128,128]{2,1,0:T(8,128)}, u32[]{:S(2)}, u32[]{:S(2)}) async-start(f32[16,128,128]{2,1,0:T(8,128)} %copy.111), calls=%async_computation.8 | async-start | bytes 2097152 | tf_op jit(solution)/shard_map/all_to_all | solution.py:21
  325.0 20.2 %all-to-all-start.10 = ((f32[32,2,128]{2,1,0:T(2,128)}), f32[32,2,128]{2,1,0:T(2,128)S(1)}, u32[]{:S(2)}, u32[]{:S(2)}) async-start(f32[32,2,128]{2,1,0:T(2,128)} %broadcast_in_dim.35), calls=%async_computation.10 | async-start | bytes 65536 | tf_op jit(solution)/shard_map/all_to_all | solution.py:28
  334.0 11.8 %copy-start.4 = (f32[1792,128]{1,0:T(8,128)S(1)}, f32[1792,128]{1,0:T(8,128)}, u32[]{:S(2)}) copy-start(f32[1792,128]{1,0:T(8,128)} %reshape.112) | copy-start | bytes 2752516
